TPU v7x, 128 devices: a whole 4x4x4 slice. The times are simulated.
128 devices in a mesh: section: 16 (over y, z_lo, core), sp: 8 (over z_hi, x).
Axes of the slice: x: 4, y: 4, z: 4 (z_hi: 2, z_lo: 2; z = z_hi * 2 + z_lo), core: 2. Of those that a mesh axis runs over, the one named last changes fastest.
Arguments:
- resid: float32 [16, 896, 6144], P('section', 'sp'), may hold values from -1.8 to 1.8
- qkv: bfloat16 [16, 896, 3, 6144], P('section', 'sp'), may hold values from -48 to 48
- cache_kv: bfloat16 [16, 2, 2, 1344, 6144], P('section', None, None, None, 'sp'), may hold values from -6 to 6
- out_proj: bfloat16 [16, 6144, 6144], P('section', 'sp'), may hold values from -0.078125 to 0.078125
- gate: float32 [16, 2, 6144], P('section'), may hold values from 0.5 to 2
- span_ids: int32 [16], P('section'), may hold values from 3 to 39
- cache_counts: int32 [16], P('section'), may hold values from 0 to 3, as said below
- span_mask: int32 [40, 40], replicated, may hold values from 0 to 1, as said below
Outputs:
- carried: float32 [16, 896, 6144], P('section', 'sp')
Inputs may be any that keep to these rules, and one draw needn't show every extreme that they name: `cache_counts`: some section has all 3 slots filled. span_mask[i][j] is 0 for j > i and 1 for j = i.
All inputs are finite; a program needn't handle non-finite values.
Results may differ from a plain program's by a relative error of at most 0.006.
Values may be sent and summed in bfloat16 or wider, within the bound.
No kernel may reach another device: no remote copies, remote signals or barrier semaphores. Data moves between devices by JAX's collectives and lax.ppermute only.
A program may use at most 384 MiB of HBM per device.

v0:
```python
import jax
import jax.numpy as jnp
from jax import lax
from jax.sharding import PartitionSpec as P

HDIM = 128
SPAN = 448
NCHUNK = 40
SLOTS = 3
VIDS = 2
TOKS = 896
KEYS = 1344


def passed_along(shard, axis, by):
    devices = lax.axis_size(axis)
    return lax.ppermute(shard, axis, [(i, (i + by) % devices) for i in range(devices)])


def visible_slots(span_id, filled, span_mask):
    row_mask = lax.dynamic_index_in_dim(span_mask, span_id, 0, keepdims=False)
    slot_ids = jnp.arange(SLOTS, dtype=jnp.int32)
    wanted = span_id - 1 - slot_ids
    columns = jnp.arange(NCHUNK, dtype=jnp.int32)
    looked = jnp.sum(jnp.where(columns[None, :] == wanted[:, None], row_mask[None, :], 0), axis=1)
    return (slot_ids < filled) & (looked == 1)


def far_scores(queries, cache_keys, live_slots):
    score_scale = HDIM ** (-0.5)
    scores = (
        jnp.einsum("qhe,khe->hqk", queries, cache_keys, preferred_element_type=jnp.float32)
        * score_scale
    )
    key_live = jnp.repeat(live_slots, SPAN)
    result = jnp.where(key_live[None, None, :], scores, -jnp.inf)
    return result


def mix_video(far_part, queries, own_keys, own_values, cache_values):
    score_scale = HDIM ** (-0.5)
    near_part = (
        jnp.einsum("qhe,khe->hqk", queries, own_keys, preferred_element_type=jnp.float32)
        * score_scale
    )
    scores = jnp.concatenate([far_part, near_part], axis=2)
    highest = jnp.max(scores, axis=2, keepdims=True)
    raised = jnp.exp(scores - highest)
    weights = (raised / jnp.sum(raised, axis=2, keepdims=True)).astype(jnp.bfloat16)
    values_all = jnp.concatenate([cache_values, own_values], axis=0)
    mixed = jnp.einsum("hqk,khe->qhe", weights, values_all, preferred_element_type=jnp.float32)
    return mixed.astype(jnp.bfloat16).reshape(SPAN, queries.shape[1] * HDIM)


def per_device(resid, qkv, cache_kv, out_proj, gate, span_ids, cache_counts, span_mask):
    own_rows = resid.shape[1]
    local_width = cache_kv.shape[4]
    local_heads = local_width // HDIM
    filled = cache_counts[0]
    live_slots = visible_slots(span_ids[0], filled, span_mask)
    cache_keys = cache_kv[0, 0].reshape(VIDS, KEYS, local_heads, HDIM)
    cache_values = cache_kv[0, 1].reshape(VIDS, KEYS, local_heads, HDIM)

    def score_video(inputs_one):
        return far_scores(inputs_one[0], inputs_one[1], live_slots)

    spread = lax.all_to_all(qkv[0], "sp", split_axis=2, concat_axis=0, tiled=True)
    queries = spread[:, 0].reshape(VIDS, SPAN, local_heads, HDIM)
    far_all = lax.map(score_video, (queries, cache_keys))
    own_keys = spread[:, 1].reshape(VIDS, SPAN, local_heads, HDIM)
    own_values = spread[:, 2].reshape(VIDS, SPAN, local_heads, HDIM)

    def mix_one(inputs_one):
        return mix_video(inputs_one[0], inputs_one[1], inputs_one[2], inputs_one[3], inputs_one[4])

    heads_all = lax.map(mix_one, (far_all, queries, own_keys, own_values, cache_values)).reshape(
        TOKS, local_width
    )
    partial = jnp.dot(heads_all, out_proj[0], preferred_element_type=jnp.float32)
    devices = lax.axis_size("sp")
    shares = partial.astype(jnp.bfloat16).reshape(devices, own_rows, partial.shape[1])
    shares = lax.all_to_all(shares, "sp", 0, 0, tiled=True)
    projected = jnp.sum(shares.astype(jnp.float32), axis=0)
    device_place = lax.axis_index("sp")
    video_of = (device_place * own_rows + jnp.arange(own_rows, dtype=jnp.int32)) // SPAN
    picker = (video_of[:, None] == jnp.arange(VIDS, dtype=jnp.int32)[None, :]).astype(jnp.float32)
    gains = jnp.dot(picker, gate[0], precision=lax.Precision.HIGHEST)
    layer_out = resid[0] + gains * projected
    return passed_along(layer_out[None], "section", 1)


def solution(mesh):
    in_specs = (
        P("section", "sp", None),
        P("section", "sp", None, None),
        P("section", None, None, None, "sp"),
        P("section", "sp", None),
        P("section", None, None),
        P("section"),
        P("section"),
        P(),
    )
    out_specs = P("section", "sp", None)
    return jax.shard_map(
        per_device, mesh=mesh, in_specs=in_specs, out_specs=out_specs, check_vma=False
    )
```

profile of v0, /device:TPU:6, one launch (start us, length us, event | category | flops | bytes accessed | tf_op | source)
XLA Modules:
  0.0 466.9 jit_solution(14958061917673568924)
XLA Ops:
  0.0 0.0 copy-start
  0.0 10.0 %copy.53 = bf16[1,112,3,6144]{1,2,3,0:T(4,128)(2,1)} copy(bf16[1,112,3,6144]{3,1,2,0:T(8,128)(2,1)} %param.13) | data formatting | bytes 8257536 | tf_op args[1]
  10.0 8.1 %all-to-all-start = ((bf16[112,3,6144]{0,1,2:T(4,128)(2,1)}), bf16[112,3,6144]{0,1,2:T(4,128)(2,1)}, u32[]{:S(2)}, u32[]{:S(2)}) async-start(bf16[112,3,6144]{0,1,2:T(4,128)(2,1)} %bitcast.82), calls=%async_computation | async-start | bytes 12582912 | tf_op jit(solution)/shard_map/all_to_all | solution.py:67
  19.4 5.7 %fusion.30 = (bf16[1,1,2,1344,768]{4,3,2,1,0:T(8,128)(2,1)}, bf16[1,1,2,1344,768]{4,3,2,1,0:T(8,128)(2,1)}) fusion(bf16[1,2,2,1344,768]{4,3,2,1,0:T(8,128)(2,1)} %param.14), kind=kLoop, calls=%fused_computation.45 | loop fusion | bytes 16515072 | tf_op jit(solution)/shard_map/slice | solution.py:61
  25.1 6.4 %copy.58 = bf16[1,1,2,1344,768]{3,4,2,1,0:T(8,128)(2,1)} copy(bf16[1,1,2,1344,768]{4,3,2,1,0:T(8,128)(2,1)} %get-tuple-element.147) | data formatting | bytes 8257536 | tf_op jit(solution)/shard_map/slice | solution.py:61
  31.5 6.4 %copy.60 = bf16[2,1344,6,128]{3,1,2,0:T(8,128)(2,1)} copy(bf16[2,1344,6,128]{1,3,2,0:T(8,128)(2,1)} %bitcast.83) | data formatting | bytes 8257536 | tf_op jit(solution)/shard_map/while | solution.py:69
  38.0 6.4 %copy.52 = bf16[1,1,2,1344,768]{3,4,2,1,0:T(8,128)(2,1)} copy(bf16[1,1,2,1344,768]{4,3,2,1,0:T(8,128)(2,1)} %get-tuple-element.148) | data formatting | bytes 8257536 | tf_op jit(solution)/shard_map/slice | solution.py:62
  44.4 6.4 %copy.62 = bf16[2,1344,6,128]{3,1,2,0:T(8,128)(2,1)} copy(bf16[2,1344,6,128]{1,3,2,0:T(8,128)(2,1)} %bitcast.84) | data formatting | bytes 8257536 | tf_op jit(solution)/shard_map/while | solution.py:76
  50.8 0.7 dynamic-slice_bitcast_fusion.3
  51.5 0.2 select_reduce_fusion
  51.7 59.1 %all-to-all-done = bf16[112,3,6144]{0,1,2:T(4,128)(2,1)} async-done(((bf16[112,3,6144]{0,1,2:T(4,128)(2,1)}), bf16[112,3,6144]{0,1,2:T(4,128)(2,1)}, u32[]{:S(2)}, u32[]{:S(2)}) %all-to-all-start) | async-done | bytes 4128800 | tf_op jit(solution)/shard_map/all_to_all | solution.py:67
  110.8 10.0 %copy.68 = bf16[112,3,8,768]{3,0,2,1:T(8,128)(2,1)} copy(bf16[112,3,8,768]{0,1,3,2:T(4,128)(2,1)} %bitcast.14) | data formatting | bytes 8257536 | tf_op jit(solution)/shard_map/all_to_all | solution.py:67
  120.8 3.5 fusion.31
  124.3 2.5 reshape.36
  126.8 1.7 copy.59
  128.5 18.3 %while.20 = (s32[]{:T(128)}, f32[2,6,448,1344]{3,2,1,0:T(8,128)}, pred[3]{0:T(512)(128)(4,1)S(1)}, bf16[2,448,6,128]{3,1,2,0:T(8,128)(2,1)S(1)}, bf16[2,1344,6,128]{3,1,2,0:T(8,128)(2,1)}, /*index=5*/s32[]{:T(128)}) while((s32[]{:T(128)}, f32[2,6,448,1344]{3,2,1,0:T(8,128)}, pred[3]{0:T(512)(128)(4,1)S(1)}, ...), condition=%wide.region_2.3_spmd, body=%wide.region_1.2_spmd.sunk | while | flops 932069376 | bytes 17899016 | solution.py:69
  128.5 0.1 broadcast_in_dim.71
  128.6 0.1 broadcast_in_dim.72
  128.7 8.9 %bitcast_dynamic-update-slice_fusion.2 = f32[2,6,448,1344]{3,2,1,0:T(8,128)} fusion(f32[2,6,448,1344]{3,2,1,0:T(8,128)} %get-tuple-element.241, s32[]{:T(128)} %get-tuple-element.240, pred[1344]{0:T(1024)(128)(4,1)S(1)} %broadcast_in_dim.72, bf16[2,1344,6,128]{3,1,2,0:T(8,128)(2,1)} %get-tuple-element.250, ...), kind=kOutput, calls=%fused_computation.clone.1 | convolution fusion | flops 932069376 | bytes 17894912 | tf_op jit(solution)/shard_map/while/body/eval_jaxpr/qhe,khe->hqk/dot_general | solution.py:32
  137.6 0.1 broadcast_in_dim.71
  137.7 0.1 broadcast_in_dim.72
  137.8 9.0 %bitcast_dynamic-update-slice_fusion.2 = f32[2,6,448,1344]{3,2,1,0:T(8,128)} fusion(f32[2,6,448,1344]{3,2,1,0:T(8,128)} %get-tuple-element.241, s32[]{:T(128)} %get-tuple-element.240, pred[1344]{0:T(1024)(128)(4,1)S(1)} %broadcast_in_dim.72, bf16[2,1344,6,128]{3,1,2,0:T(8,128)(2,1)} %get-tuple-element.250, ...), kind=kOutput, calls=%fused_computation.clone.1 | convolution fusion | flops 932069376 | bytes 17894912 | tf_op jit(solution)/shard_map/while/body/eval_jaxpr/qhe,khe->hqk/dot_general | solution.py:32
  146.8 4.1 reshape.34
  151.0 2.8 copy.63
  153.8 2.5 reshape.35
  156.3 2.8 copy.65
  159.1 81.1 %while.21 = (s32[]{:T(128)}, bf16[2,448,768]{2,1,0:T(8,128)(2,1)}, bf16[2,1344,6,128]{3,1,2,0:T(8,128)(2,1)}, bf16[2,448,6,128]{3,1,2,0:T(8,128)(2,1)}, f32[2,6,...) while((s32[]{:T(128)}, bf16[2,448,768]{2,1,0:T(8,128)(2,1)}, ...), condition=%wide.region_7.8_spmd, body=%wide.region_3.7_spmd.sunk | while | flops 1586989824 | bytes 108822680 | solution.py:76
  159.1 4.4 fusion.42
  163.5 11.6 %dynamic-slice_reduce_fusion.2 = (f32[6,448]{1,0:T(8,128)S(1)}, f32[6,448,1344]{2,1,0:T(8,128)}) fusion(f32[2,6,448,1344]{3,2,1,0:T(8,128)} %get-tuple-element.272, s32[]{:T(128)} %get-tuple-element.260), kind=kLoop, calls=%fused_computation.9.clone.1 | loop fusion | flops 3609984 | bytes 28912132 | tf_op jit(solution)/shard_map/while/body/eval_jaxpr/reduce_max | solution.py:47
  175.1 0.0 copy-start.1
  175.1 10.8 %fusion.43 = f32[6,448]{1,0:T(8,128)S(1)} fusion(f32[6,448,448]{2,1,0:T(8,128)} %get-tuple-element.230, f32[6,448,1344]{2,1,0:T(8,128)} %get-tuple-element.231, f32[6,448]{1,0:T(8,128)S(1)} %reduce_max.27), kind=kLoop, calls=%fused_computation.11.clone.1 | loop fusion | flops 14448000 | bytes 19289088 | tf_op jit(solution)/shard_map/while/body/eval_jaxpr/reduce_sum | solution.py:49
  185.9 0.0 copy-start.2
  185.9 0.0 copy-done.1
  185.9 0.1 dynamic-slice_bitcast_fusion.7
  186.1 1.2 copy-done.2
  187.2 0.9 dynamic-slice_bitcast_fusion.6
  188.1 10.0 %fusion.44 = bf16[448,6,128]{2,0,1:T(8,128)(2,1)S(1)} fusion(bf16[448,6,128]{2,0,1:T(8,128)(2,1)} %dynamic-slice_bitcast_fusion.6, bf16[1344,6,128]{2,0,1:T(8,128)(2,1)S(1)} %dynamic-slice_bitcast_fusion.7, f32[6,448,448]{2,1,0:T(8,128)} %get-tuple-element.230, f32[6,448,1344]{2,1,0:T(8,128)} %get-tuple-element.231, f32[6,448]{1,0:T(8,128)S(1)} %fusion.43, ...), kind=kOutput, calls=%fused_computation.19.clone.1 | convolution fusion | flops 1258242048 | bytes 22729728 | tf_op jit(solution)/shard_map/while/body/eval_jaxpr/hqk,khe->qhe/dot_general | solution.py:51
  198.2 0.3 copy.79
  198.4 0.3 copy.80
  198.7 0.9 constant_dynamic-update-slice_fusion.2
  199.6 4.4 fusion.42
  204.0 11.6 %dynamic-slice_reduce_fusion.2 = (f32[6,448]{1,0:T(8,128)S(1)}, f32[6,448,1344]{2,1,0:T(8,128)}) fusion(f32[2,6,448,1344]{3,2,1,0:T(8,128)} %get-tuple-element.272, s32[]{:T(128)} %get-tuple-element.260), kind=kLoop, calls=%fused_computation.9.clone.1 | loop fusion | flops 3609984 | bytes 28912132 | tf_op jit(solution)/shard_map/while/body/eval_jaxpr/reduce_max | solution.py:47
  215.6 0.0 copy-start.1
  215.6 10.8 %fusion.43 = f32[6,448]{1,0:T(8,128)S(1)} fusion(f32[6,448,448]{2,1,0:T(8,128)} %get-tuple-element.230, f32[6,448,1344]{2,1,0:T(8,128)} %get-tuple-element.231, f32[6,448]{1,0:T(8,128)S(1)} %reduce_max.27), kind=kLoop, calls=%fused_computation.11.clone.1 | loop fusion | flops 14448000 | bytes 19289088 | tf_op jit(solution)/shard_map/while/body/eval_jaxpr/reduce_sum | solution.py:49
  226.4 0.0 copy-start.2
  226.4 0.0 copy-done.1
  226.4 0.1 dynamic-slice_bitcast_fusion.7
  226.6 1.2 copy-done.2
  227.8 0.9 dynamic-slice_bitcast_fusion.6
  228.6 10.0 %fusion.44 = bf16[448,6,128]{2,0,1:T(8,128)(2,1)S(1)} fusion(bf16[448,6,128]{2,0,1:T(8,128)(2,1)} %dynamic-slice_bitcast_fusion.6, bf16[1344,6,128]{2,0,1:T(8,128)(2,1)S(1)} %dynamic-slice_bitcast_fusion.7, f32[6,448,448]{2,1,0:T(8,128)} %get-tuple-element.230, f32[6,448,1344]{2,1,0:T(8,128)} %get-tuple-element.231, f32[6,448]{1,0:T(8,128)S(1)} %fusion.43, ...), kind=kOutput, calls=%fused_computation.19.clone.1 | convolution fusion | flops 1258242048 | bytes 22729728 | tf_op jit(solution)/shard_map/while/body/eval_jaxpr/hqk,khe->qhe/dot_general | solution.py:51
  238.7 0.3 copy.79
  239.0 0.3 copy.80
  239.2 0.9 constant_dynamic-update-slice_fusion.2
  240.1 15.2 %convolution_convert_fusion = bf16[896,6144]{1,0:T(8,128)(2,1)} fusion(bf16[896,768]{1,0:T(8,128)(2,1)} %bitcast.87, bf16[1,768,6144]{2,1,0:T(8,128)(2,1)} %param.15), kind=kOutput, calls=%fused_computation.30 | convolution fusion | flops 8461221888 | bytes 21823488 | tf_op jit(solution)/shard_map/dot_general | solution.py:79
  255.4 6.9 %all-to-all-start.1 = ((bf16[8,112,6144]{2,1,0:T(8,128)(2,1)}), bf16[8,112,6144]{2,1,0:T(8,128)(2,1)}, u32[]{:S(2)}, u32[]{:S(2)}) async-start(bf16[8,112,6144]{2,1,0:T(8,128)(2,1)} %bitcast.86), calls=%async_computation.1 | async-start | bytes 22020096 | tf_op jit(solution)/shard_map/all_to_all | solution.py:82
  262.3 0.0 copy-start.3
  262.3 160.4 %all-to-all-done.1 = bf16[8,112,6144]{2,1,0:T(8,128)(2,1)} async-done(((bf16[8,112,6144]{2,1,0:T(8,128)(2,1)}), bf16[8,112,6144]{2,1,0:T(8,128)(2,1)}, u32[]{:S(2)}, u32[]{:S(2)}) %all-to-all-start.1) | async-done | bytes 11010080 | tf_op jit(solution)/shard_map/all_to_all | solution.py:82
  422.7 6.4 %convert_reduce_fusion = f32[112,6144]{1,0:T(8,128)S(1)} fusion(bf16[8,112,6144]{2,1,0:T(8,128)(2,1)} %all-to-all-done.1), kind=kLoop, calls=%fused_computation.29 | loop fusion | flops 10321920 | bytes 13762560 | tf_op jit(solution)/shard_map/reduce_sum | solution.py:83
  429.1 0.0 copy-done
  429.1 0.0 copy-done.3
  429.1 1.6 fusion.26
  430.7 0.1 collective-permute-start
  430.8 34.6 %collective-permute-done = f32[1,112,6144]{2,1,0:T(8,128)S(1)} collective-permute-done((f32[1,112,6144]{2,1,0:T(8,128)S(1)}, f32[1,112,6144]{2,1,0:T(8,128)S(1)}, u32[]{:S(2)}, u32[]{:S(2)}) %collective-permute-start) | collective-permute-done | bytes 2752544 | tf_op jit(solution)/shard_map/ppermute | solution.py:17
  465.4 1.5 copy.100
  (7 shorter events, 0.0 us)
Async XLA Ops:
  0.0 429.1 %copy-start = (f32[1,2,6144]{2,1,0:T(2,128)S(1)}, f32[1,2,6144]{2,1,0:T(2,128)}, u32[]{:S(2)}) copy-start(f32[1,2,6144]{2,1,0:T(2,128)} %param.16) | copy-start | bytes 147460
  10.0 100.8 %all-to-all-start = ((bf16[112,3,6144]{0,1,2:T(4,128)(2,1)}), bf16[112,3,6144]{0,1,2:T(4,128)(2,1)}, u32[]{:S(2)}, u32[]{:S(2)}) async-start(bf16[112,3,6144]{0,1,2:T(4,128)(2,1)} %bitcast.82), calls=%async_computation | async-start | bytes 12582912 | tf_op jit(solution)/shard_map/all_to_all | solution.py:67
  175.1 10.8 %copy-start.1 = (bf16[2,1344,6,128]{3,1,2,0:T(8,128)(2,1)S(1)}, bf16[2,1344,6,128]{3,1,2,0:T(8,128)(2,1)}, u32[]{:S(2)}) copy-start(bf16[2,1344,6,128]{3,1,2,0:T(8,128)(2,1)} %get-tuple-element.270) | copy-start | bytes 12386308 | tf_op jit(solution)/shard_map/while
  185.9 1.3 copy-start.2
  215.6 10.8 %copy-start.1 = (bf16[2,1344,6,128]{3,1,2,0:T(8,128)(2,1)S(1)}, bf16[2,1344,6,128]{3,1,2,0:T(8,128)(2,1)}, u32[]{:S(2)}) copy-start(bf16[2,1344,6,128]{3,1,2,0:T(8,128)(2,1)} %get-tuple-element.270) | copy-start | bytes 12386308 | tf_op jit(solution)/shard_map/while
  226.4 1.3 copy-start.2
  255.4 167.3 %all-to-all-start.1 = ((bf16[8,112,6144]{2,1,0:T(8,128)(2,1)}), bf16[8,112,6144]{2,1,0:T(8,128)(2,1)}, u32[]{:S(2)}, u32[]{:S(2)}) async-start(bf16[8,112,6144]{2,1,0:T(8,128)(2,1)} %bitcast.86), calls=%async_computation.1 | async-start | bytes 22020096 | tf_op jit(solution)/shard_map/all_to_all | solution.py:82
  262.3 166.8 %copy-start.3 = (f32[1,112,6144]{2,1,0:T(8,128)S(1)}, f32[1,112,6144]{2,1,0:T(8,128)}, u32[]{:S(2)}) copy-start(f32[1,112,6144]{2,1,0:T(8,128)} %param.12) | copy-start | bytes 8257540
  430.7 34.7 %collective-permute-start = (f32[1,112,6144]{2,1,0:T(8,128)S(1)}, f32[1,112,6144]{2,1,0:T(8,128)S(1)}, u32[]{:S(2)}, u32[]{:S(2)}) collective-permute-start(f32[1,112,6144]{2,1,0:T(8,128)S(1)} %fusion.26), channel_id=1, source_target_pairs={{0,8},{8,16},{16,24},{24,32},{32,40},{40,48},{48,56},{56,64},{64,7... | collective-permute-start | bytes 8257544 | tf_op jit(solution)/shard_map/ppermute | solution.py:17
where the time goes:
time: 469 us; the launch traced here: 467 us
  waiting for transfers between devices  254 us (54%)
  local copies, waits for them, and re-layouts  81.3 us (17%)
  matrix products  63.6 us (14%)
  other arithmetic  51.5 us (11%)
  starting transfers between devices  15.1 us (3%)
    all_to_all x1, waiting for transfers between devices, per_device(): shares = lax.all_to_all(shares, 'sp', 0, 0, tiled=True)  160 us
    all_to_all x1, waiting for transfers between devices, per_device(): lax.all_to_all(qkv[0], 'sp', split_axis=2, concat_axis=0, tiled=True)  59.1 us
    ppermute x1, waiting for transfers between devices, passed_along(): lax.ppermute(shard, axis, [(i, (i + by) % devices) for i in range(devices)])  34.6 us
    reduce_max x4, other arithmetic, mix_video(): highest = jnp.max(scores, axis=2, keepdims=True)  23.2 us
    reduce_sum x2, other arithmetic, mix_video(): jnp.sum(raised, axis=2, keepdims=True)  21.6 us
    dot_general x2, matrix products, mix_video(): jnp.einsum('hqk,khe->qhe', weights, values_all, preferred_element_type=jn...  20.1 us
    dot_general x2, matrix products, far_scores(): jnp.einsum('qhe,khe->hqk', queries, cache_keys, preferred_element_type=jn...  18 us
    dot_general x1, matrix products, per_device(): jnp.dot(heads_all, out_proj[0], preferred_element_type=jnp.float32)  15.2 us
  transfers between devices with their start and end apart: 3, of which 3 were waited for; matrix products, arithmetic and copies ran while one was open for 7% of the time, Pallas kernels for 0%

commit v1 on v0

--- a/solution.py
+++ b/solution.py
@@ -64,7 +64,10 @@
     def score_video(inputs_one):
         return far_scores(inputs_one[0], inputs_one[1], live_slots)
 
-    spread = lax.all_to_all(qkv[0], "sp", split_axis=2, concat_axis=0, tiled=True)
+    spread = jnp.concatenate(
+        lax.all_to_all(jnp.stack(jnp.split(qkv[0], lax.axis_size("sp"), axis=2)), "sp", 0, 0),
+        axis=0,
+    )
     queries = spread[:, 0].reshape(VIDS, SPAN, local_heads, HDIM)
     far_all = lax.map(score_video, (queries, cache_keys))
     own_keys = spread[:, 1].reshape(VIDS, SPAN, local_heads, HDIM)

time: 469 us -> 427 us (0.910)
  waiting for transfers between devices: 254 us -> 222 us
  local copies, waits for them, and re-layouts: 81.3 us -> 72.6 us
    all_to_all x1, waiting for transfers between devices: 59.1 us -> 26.5 us  [per_device(): lax.all_to_all(jnp.stack(jnp.split(qkv[0], lax.axis_size('sp'), axis=2)),...]
    all_to_all x1, local copies, waits for them, and re-layouts: 10 us -> 2.52 us  [per_device(): lax.all_to_all(jnp.stack(jnp.split(qkv[0], lax.axis_size('sp'), axis=2)),...]
    unnamed x6 -> x14, local copies, waits for them, and re-layouts: 11.6 us -> 11.7 us
  transfers between devices with their start and end apart: 3 -> 3, of which waited for: 3 -> 3; matrix products, arithmetic and copies ran while one was open for 7% -> 8% of each run, Pallas kernels for 0% -> 0%
where the time goes in v1:
time: 427 us; the launch traced here: 426 us
  waiting for transfers between devices  222 us (52%)
  local copies, waits for them, and re-layouts  72.6 us (17%)
  matrix products  63.6 us (15%)
  other arithmetic  51.5 us (12%)
  starting transfers between devices  15.1 us (4%)
    all_to_all x1, waiting for transfers between devices, per_device(): shares = lax.all_to_all(shares, 'sp', 0, 0, tiled=True)  160 us
    ppermute x1, waiting for transfers between devices, passed_along(): lax.ppermute(shard, axis, [(i, (i + by) % devices) for i in range(devices)])  34.6 us
    all_to_all x1, waiting for transfers between devices, per_device(): lax.all_to_all(jnp.stack(jnp.split(qkv[0], lax.axis_size('sp'), axis=2)),...  26.5 us
    reduce_max x4, other arithmetic, mix_video(): highest = jnp.max(scores, axis=2, keepdims=True)  23.2 us
    reduce_sum x2, other arithmetic, mix_video(): jnp.sum(raised, axis=2, keepdims=True)  21.6 us
    dot_general x2, matrix products, mix_video(): jnp.einsum('hqk,khe->qhe', weights, values_all, preferred_element_type=jn...  20.1 us
    dot_general x2, matrix products, far_scores(): jnp.einsum('qhe,khe->hqk', queries, cache_keys, preferred_element_type=jn...  18 us
    dot_general x1, matrix products, per_device(): jnp.dot(heads_all, out_proj[0], preferred_element_type=jnp.float32)  15.2 us
  transfers between devices with their start and end apart: 3, of which 3 were waited for; matrix products, arithmetic and copies ran while one was open for 8% of the time, Pallas kernels for 0%

profile of v1, /device:TPU:6, one launch (start us, length us, event | category | flops | bytes accessed | tf_op | source)
XLA Modules:
  0.0 425.9 jit_solution(6030224219934321928)
XLA Ops:
  0.0 2.0 fusion.34
  2.0 1.8 fusion.33
  3.9 1.9 fusion.32
  5.8 1.9 fusion.31
  7.6 0.9 fusion.30
  8.5 0.9 fusion.29
  9.4 0.8 fusion.28
  10.2 0.8 fusion.27
  11.0 8.1 %all-to-all-start = ((bf16[8,112,3,768]{3,1,2,0:T(8,128)(2,1)}), bf16[8,112,3,768]{3,1,2,0:T(8,128)(2,1)}, u32[]{:S(2)}, u32[]{:S(2)}) async-start(bf16[8,112,3,768]{3,1,2,0:T(8,128)(2,1)} %fusion.27), calls=%async_computation | async-start | bytes 8257536 | tf_op jit(solution)/shard_map/all_to_all | solution.py:68
  20.4 5.7 %fusion.38 = (bf16[1,1,2,1344,768]{4,3,2,1,0:T(8,128)(2,1)}, bf16[1,1,2,1344,768]{4,3,2,1,0:T(8,128)(2,1)}) fusion(bf16[1,2,2,1344,768]{4,3,2,1,0:T(8,128)(2,1)} %param.14), kind=kLoop, calls=%fused_computation.61 | loop fusion | bytes 16515072 | tf_op jit(solution)/shard_map/slice | solution.py:61
  26.1 6.5 %copy.67 = bf16[1,1,2,1344,768]{3,4,2,1,0:T(8,128)(2,1)} copy(bf16[1,1,2,1344,768]{4,3,2,1,0:T(8,128)(2,1)} %get-tuple-element.147) | data formatting | bytes 8257536 | tf_op jit(solution)/shard_map/slice | solution.py:61
  32.5 6.5 %copy.69 = bf16[2,1344,6,128]{3,1,2,0:T(8,128)(2,1)} copy(bf16[2,1344,6,128]{1,3,2,0:T(8,128)(2,1)} %bitcast.110) | data formatting | bytes 8257536 | tf_op jit(solution)/shard_map/while | solution.py:72
  39.0 6.5 %copy.63 = bf16[1,1,2,1344,768]{3,4,2,1,0:T(8,128)(2,1)} copy(bf16[1,1,2,1344,768]{4,3,2,1,0:T(8,128)(2,1)} %get-tuple-element.148) | data formatting | bytes 8257536 | tf_op jit(solution)/shard_map/slice | solution.py:62
  45.5 6.4 %copy.71 = bf16[2,1344,6,128]{3,1,2,0:T(8,128)(2,1)} copy(bf16[2,1344,6,128]{1,3,2,0:T(8,128)(2,1)} %bitcast.111) | data formatting | bytes 8257536 | tf_op jit(solution)/shard_map/while | solution.py:79
  51.9 0.7 dynamic-slice_bitcast_fusion.3
  52.6 0.2 select_reduce_fusion
  52.8 26.5 %all-to-all-done = bf16[8,112,3,768]{3,1,2,0:T(8,128)(2,1)} async-done(((bf16[8,112,3,768]{3,1,2,0:T(8,128)(2,1)}), bf16[8,112,3,768]{3,1,2,0:T(8,128)(2,1)}, u32[]{:S(2)}, u32[]{:S(2)}) %all-to-all-start) | async-done | bytes 4128800 | tf_op jit(solution)/shard_map/all_to_all | solution.py:68
  79.4 2.5 copy.64
  81.9 1.3 fusion.39
  83.2 2.5 reshape.40
  85.7 1.7 copy.68
  87.4 18.4 %while.20 = (s32[]{:T(128)}, f32[2,6,448,1344]{3,2,1,0:T(8,128)}, pred[3]{0:T(512)(128)(4,1)S(1)}, bf16[2,448,6,128]{3,1,2,0:T(8,128)(2,1)S(1)}, bf16[2,1344,6,128]{3,1,2,0:T(8,128)(2,1)}, /*index=5*/s32[]{:T(128)}) while((s32[]{:T(128)}, f32[2,6,448,1344]{3,2,1,0:T(8,128)}, pred[3]{0:T(512)(128)(4,1)S(1)}, ...), condition=%wide.region_2.3_spmd, body=%wide.region_1.2_spmd.sunk | while | flops 932069376 | bytes 17899016 | solution.py:72
  87.4 0.1 broadcast_in_dim.71
  87.5 0.1 broadcast_in_dim.72
  87.6 9.0 %bitcast_dynamic-update-slice_fusion.2 = f32[2,6,448,1344]{3,2,1,0:T(8,128)} fusion(f32[2,6,448,1344]{3,2,1,0:T(8,128)} %get-tuple-element.241, s32[]{:T(128)} %get-tuple-element.240, pred[1344]{0:T(1024)(128)(4,1)S(1)} %broadcast_in_dim.72, bf16[2,1344,6,128]{3,1,2,0:T(8,128)(2,1)} %get-tuple-element.250, ...), kind=kOutput, calls=%fused_computation.clone.1 | convolution fusion | flops 932069376 | bytes 17894912 | tf_op jit(solution)/shard_map/while/body/eval_jaxpr/qhe,khe->hqk/dot_general | solution.py:32
  96.6 0.1 broadcast_in_dim.71
  96.6 0.1 broadcast_in_dim.72
  96.7 9.0 %bitcast_dynamic-update-slice_fusion.2 = f32[2,6,448,1344]{3,2,1,0:T(8,128)} fusion(f32[2,6,448,1344]{3,2,1,0:T(8,128)} %get-tuple-element.241, s32[]{:T(128)} %get-tuple-element.240, pred[1344]{0:T(1024)(128)(4,1)S(1)} %broadcast_in_dim.72, bf16[2,1344,6,128]{3,1,2,0:T(8,128)(2,1)} %get-tuple-element.250, ...), kind=kOutput, calls=%fused_computation.clone.1 | convolution fusion | flops 932069376 | bytes 17894912 | tf_op jit(solution)/shard_map/while/body/eval_jaxpr/qhe,khe->hqk/dot_general | solution.py:32
  105.8 4.1 reshape.38
  109.9 2.8 copy.72
  112.7 2.5 reshape.39
  115.2 2.8 copy.74
  118.0 81.0 %while.21 = (s32[]{:T(128)}, bf16[2,448,768]{2,1,0:T(8,128)(2,1)}, bf16[2,1344,6,128]{3,1,2,0:T(8,128)(2,1)}, bf16[2,448,6,128]{3,1,2,0:T(8,128)(2,1)}, f32[2,6,...) while((s32[]{:T(128)}, bf16[2,448,768]{2,1,0:T(8,128)(2,1)}, ...), condition=%wide.region_7.8_spmd, body=%wide.region_3.7_spmd.sunk | while | flops 1586989824 | bytes 108822680 | solution.py:79
  118.0 4.4 %fusion.50 = (f32[6,448]{1,0:T(8,128)S(1)}, f32[6,448,448]{2,1,0:T(8,128)}) fusion(bf16[2,448,6,128]{3,1,2,0:T(8,128)(2,1)} %get-tuple-element.274, s32[]{:T(128)} %get-tuple-element.260, bf16[2,448,6,128]{3,1,2,0:T(8,128)(2,1)S(1)} %get-tuple-element.273), kind=kOutput, calls=%fused_computation.60.clone.1 | convolution fusion | flops 310687104 | bytes 6204928 | tf_op jit(solution)/shard_map/while/body/eval_jaxpr/qhe,khe->hqk/dot_general | solution.py:43
  122.4 11.6 %dynamic-slice_reduce_fusion.2 = (f32[6,448]{1,0:T(8,128)S(1)}, f32[6,448,1344]{2,1,0:T(8,128)}) fusion(f32[2,6,448,1344]{3,2,1,0:T(8,128)} %get-tuple-element.272, s32[]{:T(128)} %get-tuple-element.260), kind=kLoop, calls=%fused_computation.9.clone.1 | loop fusion | flops 3609984 | bytes 28912132 | tf_op jit(solution)/shard_map/while/body/eval_jaxpr/reduce_max | solution.py:47
  134.0 10.8 %fusion.51 = f32[6,448]{1,0:T(8,128)S(1)} fusion(f32[6,448,448]{2,1,0:T(8,128)} %get-tuple-element.230, f32[6,448,1344]{2,1,0:T(8,128)} %get-tuple-element.231, f32[6,448]{1,0:T(8,128)S(1)} %reduce_max.27), kind=kLoop, calls=%fused_computation.11.clone.1 | loop fusion | flops 14448000 | bytes 19289088 | tf_op jit(solution)/shard_map/while/body/eval_jaxpr/reduce_sum | solution.py:49
  144.8 0.1 dynamic-slice_bitcast_fusion.7
  145.0 1.2 copy-done.2
  146.1 0.9 dynamic-slice_bitcast_fusion.6
  147.0 10.0 %fusion.52 = bf16[448,6,128]{2,0,1:T(8,128)(2,1)S(1)} fusion(bf16[448,6,128]{2,0,1:T(8,128)(2,1)} %dynamic-slice_bitcast_fusion.6, bf16[1344,6,128]{2,0,1:T(8,128)(2,1)S(1)} %dynamic-slice_bitcast_fusion.7, f32[6,448,448]{2,1,0:T(8,128)} %get-tuple-element.230, f32[6,448,1344]{2,1,0:T(8,128)} %get-tuple-element.231, f32[6,448]{1,0:T(8,128)S(1)} %fusion.51, ...), kind=kOutput, calls=%fused_computation.19.clone.1 | convolution fusion | flops 1258242048 | bytes 22729728 | tf_op jit(solution)/shard_map/while/body/eval_jaxpr/hqk,khe->qhe/dot_general | solution.py:51
  157.1 0.3 copy.86
  157.3 0.3 copy.87
  157.6 0.9 constant_dynamic-update-slice_fusion.2
  158.5 4.4 %fusion.50 = (f32[6,448]{1,0:T(8,128)S(1)}, f32[6,448,448]{2,1,0:T(8,128)}) fusion(bf16[2,448,6,128]{3,1,2,0:T(8,128)(2,1)} %get-tuple-element.274, s32[]{:T(128)} %get-tuple-element.260, bf16[2,448,6,128]{3,1,2,0:T(8,128)(2,1)S(1)} %get-tuple-element.273), kind=kOutput, calls=%fused_computation.60.clone.1 | convolution fusion | flops 310687104 | bytes 6204928 | tf_op jit(solution)/shard_map/while/body/eval_jaxpr/qhe,khe->hqk/dot_general | solution.py:43
  162.9 11.6 %dynamic-slice_reduce_fusion.2 = (f32[6,448]{1,0:T(8,128)S(1)}, f32[6,448,1344]{2,1,0:T(8,128)}) fusion(f32[2,6,448,1344]{3,2,1,0:T(8,128)} %get-tuple-element.272, s32[]{:T(128)} %get-tuple-element.260), kind=kLoop, calls=%fused_computation.9.clone.1 | loop fusion | flops 3609984 | bytes 28912132 | tf_op jit(solution)/shard_map/while/body/eval_jaxpr/reduce_max | solution.py:47
  174.5 10.8 %fusion.51 = f32[6,448]{1,0:T(8,128)S(1)} fusion(f32[6,448,448]{2,1,0:T(8,128)} %get-tuple-element.230, f32[6,448,1344]{2,1,0:T(8,128)} %get-tuple-element.231, f32[6,448]{1,0:T(8,128)S(1)} %reduce_max.27), kind=kLoop, calls=%fused_computation.11.clone.1 | loop fusion | flops 14448000 | bytes 19289088 | tf_op jit(solution)/shard_map/while/body/eval_jaxpr/reduce_sum | solution.py:49
  185.3 0.0 copy-start.2
  185.3 0.0 copy-done.1
  185.3 0.1 dynamic-slice_bitcast_fusion.7
  185.5 1.2 copy-done.2
  186.7 0.9 dynamic-slice_bitcast_fusion.6
  187.5 10.0 %fusion.52 = bf16[448,6,128]{2,0,1:T(8,128)(2,1)S(1)} fusion(bf16[448,6,128]{2,0,1:T(8,128)(2,1)} %dynamic-slice_bitcast_fusion.6, bf16[1344,6,128]{2,0,1:T(8,128)(2,1)S(1)} %dynamic-slice_bitcast_fusion.7, f32[6,448,448]{2,1,0:T(8,128)} %get-tuple-element.230, f32[6,448,1344]{2,1,0:T(8,128)} %get-tuple-element.231, f32[6,448]{1,0:T(8,128)S(1)} %fusion.51, ...), kind=kOutput, calls=%fused_computation.19.clone.1 | convolution fusion | flops 1258242048 | bytes 22729728 | tf_op jit(solution)/shard_map/while/body/eval_jaxpr/hqk,khe->qhe/dot_general | solution.py:51
  197.6 0.3 copy.86
  197.9 0.3 copy.87
  198.1 0.9 constant_dynamic-update-slice_fusion.2
  199.0 15.2 %convolution_convert_fusion = bf16[896,6144]{1,0:T(8,128)(2,1)} fusion(bf16[896,768]{1,0:T(8,128)(2,1)} %bitcast.122, bf16[1,768,6144]{2,1,0:T(8,128)(2,1)} %param.15), kind=kOutput, calls=%fused_computation.30 | convolution fusion | flops 8461221888 | bytes 21823488 | tf_op jit(solution)/shard_map/dot_general | solution.py:82
  214.3 6.9 %all-to-all-start.1 = ((bf16[8,112,6144]{2,1,0:T(8,128)(2,1)}), bf16[8,112,6144]{2,1,0:T(8,128)(2,1)}, u32[]{:S(2)}, u32[]{:S(2)}) async-start(bf16[8,112,6144]{2,1,0:T(8,128)(2,1)} %bitcast.113), calls=%async_computation.1 | async-start | bytes 22020096 | tf_op jit(solution)/shard_map/all_to_all | solution.py:85
  221.2 0.0 copy-start.4
  221.2 160.4 %all-to-all-done.1 = bf16[8,112,6144]{2,1,0:T(8,128)(2,1)} async-done(((bf16[8,112,6144]{2,1,0:T(8,128)(2,1)}), bf16[8,112,6144]{2,1,0:T(8,128)(2,1)}, u32[]{:S(2)}, u32[]{:S(2)}) %all-to-all-start.1) | async-done | bytes 11010080 | tf_op jit(solution)/shard_map/all_to_all | solution.py:85
  381.6 6.4 %convert_reduce_fusion = f32[112,6144]{1,0:T(8,128)S(1)} fusion(bf16[8,112,6144]{2,1,0:T(8,128)(2,1)} %all-to-all-done.1), kind=kLoop, calls=%fused_computation.29 | loop fusion | flops 10321920 | bytes 13762560 | tf_op jit(solution)/shard_map/reduce_sum | solution.py:86
  388.1 1.6 fusion.26
  389.7 0.1 collective-permute-start
  389.7 34.6 %collective-permute-done = f32[1,112,6144]{2,1,0:T(8,128)S(1)} collective-permute-done((f32[1,112,6144]{2,1,0:T(8,128)S(1)}, f32[1,112,6144]{2,1,0:T(8,128)S(1)}, u32[]{:S(2)}, u32[]{:S(2)}) %collective-permute-start) | collective-permute-done | bytes 2752544 | tf_op jit(solution)/shard_map/ppermute | solution.py:17
  424.3 1.5 copy.114
  (16 shorter events, 0.1 us)
Async XLA Ops:
  0.0 388.0 %copy-start = (f32[1,2,6144]{2,1,0:T(2,128)S(1)}, f32[1,2,6144]{2,1,0:T(2,128)}, u32[]{:S(2)}) copy-start(f32[1,2,6144]{2,1,0:T(2,128)} %param.16) | copy-start | bytes 147460
  0.0 7.6 %copy-start.3 = (bf16[1,112,3,6144]{3,1,2,0:T(8,128)(2,1)S(1)}, bf16[1,112,3,6144]{3,1,2,0:T(8,128)(2,1)}, u32[]{:S(2)}) copy-start(bf16[1,112,3,6144]{3,1,2,0:T(8,128)(2,1)} %param.13) | copy-start | bytes 12386308
  11.0 68.3 %all-to-all-start = ((bf16[8,112,3,768]{3,1,2,0:T(8,128)(2,1)}), bf16[8,112,3,768]{3,1,2,0:T(8,128)(2,1)}, u32[]{:S(2)}, u32[]{:S(2)}) async-start(bf16[8,112,3,768]{3,1,2,0:T(8,128)(2,1)} %fusion.27), calls=%async_computation | async-start | bytes 8257536 | tf_op jit(solution)/shard_map/all_to_all | solution.py:68
  134.0 10.8 %copy-start.1 = (bf16[2,1344,6,128]{3,1,2,0:T(8,128)(2,1)S(1)}, bf16[2,1344,6,128]{3,1,2,0:T(8,128)(2,1)}, u32[]{:S(2)}) copy-start(bf16[2,1344,6,128]{3,1,2,0:T(8,128)(2,1)} %get-tuple-element.270) | copy-start | bytes 12386308 | tf_op jit(solution)/shard_map/while
  144.8 1.3 copy-start.2
  174.5 10.8 %copy-start.1 = (bf16[2,1344,6,128]{3,1,2,0:T(8,128)(2,1)S(1)}, bf16[2,1344,6,128]{3,1,2,0:T(8,128)(2,1)}, u32[]{:S(2)}) copy-start(bf16[2,1344,6,128]{3,1,2,0:T(8,128)(2,1)} %get-tuple-element.270) | copy-start | bytes 12386308 | tf_op jit(solution)/shard_map/while
  185.3 1.3 copy-start.2
  214.3 167.4 %all-to-all-start.1 = ((bf16[8,112,6144]{2,1,0:T(8,128)(2,1)}), bf16[8,112,6144]{2,1,0:T(8,128)(2,1)}, u32[]{:S(2)}, u32[]{:S(2)}) async-start(bf16[8,112,6144]{2,1,0:T(8,128)(2,1)} %bitcast.113), calls=%async_computation.1 | async-start | bytes 22020096 | tf_op jit(solution)/shard_map/all_to_all | solution.py:85
  221.2 166.9 %copy-start.4 = (f32[1,112,6144]{2,1,0:T(8,128)S(1)}, f32[1,112,6144]{2,1,0:T(8,128)}, u32[]{:S(2)}) copy-start(f32[1,112,6144]{2,1,0:T(8,128)} %param.12) | copy-start | bytes 8257540
  389.7 34.7 %collective-permute-start = (f32[1,112,6144]{2,1,0:T(8,128)S(1)}, f32[1,112,6144]{2,1,0:T(8,128)S(1)}, u32[]{:S(2)}, u32[]{:S(2)}) collective-permute-start(f32[1,112,6144]{2,1,0:T(8,128)S(1)} %fusion.26), channel_id=1, source_target_pairs={{0,8},{8,16},{16,24},{24,32},{32,40},{40,48},{48,56},{56,64},{64,7... | collective-permute-start | bytes 8257544 | tf_op jit(solution)/shard_map/ppermute | solution.py:17
